TPU v7x, 512 devices: a whole 4x4x16 slice. The times are simulated.
512 devices in a mesh: fibre: 32 (over z, core), group: 16 (over y, x).
Axes of the slice: x: 4, y: 4, z: 16, core: 2. Of those that a mesh axis runs over, the one named last changes fastest.
Arguments:
- species_field: float32 [512, 524288], P('fibre', 'group'), may hold values from -45 to 45, as said below
- start_block: float32 [512, 64], replicated, may hold values from -4 to 4
Outputs:
- mode_basis: float32 [512, 64], replicated
- core_tensor: float32 [64, 524288], P(None, ('group', 'fibre'))
Inputs may be any that keep to these rules, and one draw needn't show every extreme that they name: `species_field`: float32 field values.
All inputs are finite; a program needn't handle non-finite values.
Results may differ from a plain program's by a relative error of at most 0.0003.
Values sent between devices are 32-bit elements; how exact they have to be, the bound alone decides.
No kernel may reach another device: no remote copies, remote signals or barrier semaphores. Data moves between devices by JAX's collectives and lax.ppermute only.
A program may use at most 64 MiB of HBM per device.

v0:
```python
import jax
import jax.numpy as jnp
from jax import lax
from jax.sharding import PartitionSpec as P

ITERS = 3
highest_precision = lax.Precision.HIGHEST


def orthonormal(matrix):
    inner_gram = jnp.dot(matrix.T, matrix, precision=highest_precision)
    lower_factor = jnp.linalg.cholesky(inner_gram)
    return lax.linalg.triangular_solve(
        lower_factor, matrix, left_side=False, lower=True, transpose_a=True
    )


def on_device(species_field, start_block):
    fibres = lax.all_to_all(species_field, "fibre", split_axis=1, concat_axis=0, tiled=True)
    total_columns = fibres.shape[1] * lax.axis_size("fibre") * lax.axis_size("group")
    mode_basis = orthonormal(start_block)
    local_gram = jnp.dot(fibres, fibres.T, precision=highest_precision) / total_columns
    gram_matrix = lax.psum(local_gram, ("fibre", "group"))
    for iteration in range(ITERS):
        mode_basis = orthonormal(jnp.dot(gram_matrix, mode_basis, precision=highest_precision))
    core_tensor = jnp.dot(mode_basis.T, fibres, precision=highest_precision)
    return (mode_basis, core_tensor)


def solution(mesh):
    placed = (P("fibre", "group"), P())
    return jax.shard_map(
        on_device,
        mesh=mesh,
        in_specs=placed,
        out_specs=(P(), P(None, ("group", "fibre"))),
        check_vma=False,
    )
```

profile of v0, /device:TPU:1, one launch (start us, length us, event | category | flops | bytes accessed | tf_op | source)
XLA Modules:
  0.0 643.5 jit_solution(7276870236529994059)
XLA Ops:
  7.2 0.0 copy-start
  7.2 3.2 copy.24
  10.4 16.7 %all-to-all-start = ((f32[16,32,1024]{2,0,1:T(8,128)}), f32[16,32,1024]{2,0,1:T(8,128)S(1)}, u32[]{:S(2)}, u32[]{:S(2)}) async-start(f32[16,32,1024]{2,0,1:T(8,128)} %bitcast.75), calls=%async_computation | async-start | bytes 4194304 | tf_op jit(solution)/shard_map/all_to_all | solution.py:19
  27.2 0.0 all-reduce.2.cloned.1.call-start
  27.2 0.0 copy-done
  27.2 0.3 fusion.18
  27.5 0.1 copy.18
  27.6 5.8 cholesky.74
  33.5 92.3 %all-to-all-done = f32[16,32,1024]{2,0,1:T(8,128)S(1)} async-done(((f32[16,32,1024]{2,0,1:T(8,128)}), f32[16,32,1024]{2,0,1:T(8,128)S(1)}, u32[]{:S(2)}, u32[]{:S(2)}) %all-to-all-start) | async-done | bytes 2097184 | tf_op jit(solution)/shard_map/all_to_all | solution.py:19
  125.8 4.6 convolution_multiply_fusion
  130.3 0.0 all-reduce.2.cloned.1.call-update
  130.4 0.6 compare_reduce_fusion.3
  131.0 0.7 fusion
  131.6 4.9 custom-call.8
  136.5 0.3 convolution_bitcast_fusion.3
  136.9 454.4 %all-reduce.2.cloned.1.call-done = f32[512,512]{1,0:T(8,128)} async-done(((f32[512,512]{1,0:T(8,128)}), f32[512,512]{1,0:T(8,128)}) %all-reduce.2.cloned.1.call-update) | async-done | bytes 1048592 | tf_op jit(solution)/shard_map/psum | solution.py:23
  591.3 0.0 copy-start.1
  591.3 2.4 fusion.19
  593.7 0.3 fusion.20
  594.0 0.1 copy.19
  594.1 5.8 cholesky.85
  600.0 0.6 compare_reduce_fusion.2
  600.6 0.7 fusion.1
  601.3 4.9 custom-call.9
  606.2 0.3 convolution_bitcast_fusion.2
  606.5 0.0 copy-done.1
  606.5 1.1 fusion.21
  607.6 0.3 fusion.22
  607.9 0.1 copy.20
  608.0 5.8 cholesky.96
  613.9 0.6 compare_reduce_fusion.1
  614.5 0.7 fusion.2
  615.2 4.9 custom-call.10
  620.1 0.3 convolution_bitcast_fusion.1
  620.4 1.3 fusion.23
  621.8 0.3 fusion.24
  622.0 0.1 copy.21
  622.1 5.8 cholesky.107
  628.0 0.6 compare_reduce_fusion
  628.6 0.7 fusion.3
  629.3 4.9 custom-call.11
  634.2 0.3 convolution_bitcast_fusion
  634.5 0.0 copy-start.2
  634.6 2.1 fusion.25
  636.6 0.0 copy-done.2
  (8 shorter events, 0.2 us)
Async XLA Ops:
  7.2 20.0 %copy-start = (f32[512,64]{0,1:T(8,128)S(1)}, f32[512,64]{0,1:T(8,128)}, u32[]{:S(2)}) copy-start(f32[512,64]{0,1:T(8,128)} %param.6) | copy-start | bytes 393220
  10.4 115.4 %all-to-all-start = ((f32[16,32,1024]{2,0,1:T(8,128)}), f32[16,32,1024]{2,0,1:T(8,128)S(1)}, u32[]{:S(2)}, u32[]{:S(2)}) async-start(f32[16,32,1024]{2,0,1:T(8,128)} %bitcast.75), calls=%async_computation | async-start | bytes 4194304 | tf_op jit(solution)/shard_map/all_to_all | solution.py:19
  27.2 564.1 %all-reduce.2.cloned.1.call-start = ((), (), s32[]{:S(2)}) async-start(), calls=%async_computation.1 | async-start | bytes 2097152 | tf_op jit(solution)/shard_map/psum | solution.py:23
  591.3 15.2 %copy-start.1 = (f32[512,512]{1,0:T(8,128)S(1)}, f32[512,512]{1,0:T(8,128)}, u32[]{:S(2)}) copy-start(f32[512,512]{1,0:T(8,128)} %all-reduce.2.cloned.1.call-done) | copy-start | bytes 3145732
  634.5 2.1 copy-start.2
Sparse Core Ops, SparseCore 0:
  130.5 460.7 all-reduce.1
where the time goes:
time: 644 us; the launch traced here: 643 us
  waiting for transfers between devices  547 us (85%)
  other arithmetic  48.3 us (8%)
  starting transfers between devices  16.8 us (3%)
  between operations  14.2 us (2%)
  matrix products  13.9 us (2%)
    psum x1, waiting for transfers between devices, on_device(): gram_matrix = lax.psum(local_gram, ('fibre', 'group'))  454 us
    all_to_all x1, waiting for transfers between devices, on_device(): lax.all_to_all(species_field, 'fibre', split_axis=1, concat_axis=0, tiled...  92.3 us
    another operation x12, other arithmetic, orthonormal(): lower_factor = jnp.linalg.cholesky(inner_gram)  26.1 us
    another operation x8, other arithmetic, orthonormal(): lax.linalg.triangular_solve(lower_factor, matrix, left_side=False, lower=...  22.2 us
    all_to_all x1, starting transfers between devices, on_device(): lax.all_to_all(species_field, 'fibre', split_axis=1, concat_axis=0, tiled...  16.7 us
  transfers between devices with their start and end apart: 2, of which 2 were waited for; matrix products, arithmetic and copies ran while one was open for 2% of the time, Pallas kernels for 0%

commit v1 on v0

--- a/solution.py
+++ b/solution.py
@@ -20,7 +20,7 @@
     total_columns = fibres.shape[1] * lax.axis_size("fibre") * lax.axis_size("group")
     mode_basis = orthonormal(start_block)
     local_gram = jnp.dot(fibres, fibres.T, precision=highest_precision) / total_columns
-    gram_matrix = lax.psum(local_gram, ("fibre", "group"))
+    gram_matrix = lax.psum(lax.psum(local_gram, "group"), "fibre")
     for iteration in range(ITERS):
         mode_basis = orthonormal(jnp.dot(gram_matrix, mode_basis, precision=highest_precision))
     core_tensor = jnp.dot(mode_basis.T, fibres, precision=highest_precision)

time: 644 us -> 505 us (0.78)
  waiting for transfers between devices: 547 us -> 309 us
  blocking collectives: 0 us -> 117 us
  starting transfers between devices: 16.8 us -> 0.26 us
    psum x1 -> x2, waiting for transfers between devices: 454 us -> 308 us  [on_device(): gram_matrix = lax.psum(lax.psum(local_gram, 'group'), 'fibre')]
    all_to_all x0 -> x1, blocking collectives: none -> 117 us  [on_device(): lax.all_to_all(species_field, 'fibre', split_axis=1, concat_axis=0, tiled...]
    all_to_all x1 -> x0, waiting for transfers between devices: 92.3 us -> none  [on_device(): lax.all_to_all(species_field, 'fibre', split_axis=1, concat_axis=0, tiled...]
    all_to_all x1 -> x0, starting transfers between devices: 16.7 us -> none  [on_device(): lax.all_to_all(species_field, 'fibre', split_axis=1, concat_axis=0, tiled...]
  transfers between devices with their start and end apart: 2 -> 2, of which waited for: 2 -> 2; matrix products, arithmetic and copies ran while one was open for 2% -> 3% of each run, Pallas kernels for 0% -> 0%
where the time goes in v1:
time: 505 us; the launch traced here: 504 us
  waiting for transfers between devices  309 us (61%)
  blocking collectives  117 us (23%)
  other arithmetic  48.3 us (10%)
  between operations  14.2 us (3%)
  matrix products  13.8 us (3%)
    psum x2, waiting for transfers between devices, on_device(): gram_matrix = lax.psum(lax.psum(local_gram, 'group'), 'fibre')  308 us
    all_to_all x1, blocking collectives, on_device(): lax.all_to_all(species_field, 'fibre', split_axis=1, concat_axis=0, tiled...  117 us
    another operation x12, other arithmetic, orthonormal(): lower_factor = jnp.linalg.cholesky(inner_gram)  26.1 us
    another operation x8, other arithmetic, orthonormal(): lax.linalg.triangular_solve(lower_factor, matrix, left_side=False, lower=...  22.2 us
  transfers between devices with their start and end apart: 2, of which 2 were waited for; matrix products, arithmetic and copies ran while one was open for 3% of the time, Pallas kernels for 0%

profile of v1, /device:TPU:1, one launch (start us, length us, event | category | flops | bytes accessed | tf_op | source)
XLA Modules:
  0.0 504.4 jit_solution(1205673229309258222)
XLA Ops:
  7.2 0.0 copy-start
  7.2 0.0 all-reduce.3.cloned.1.call-start
  7.2 1.8 copy.24
  9.0 117.2 %all_to_all.19 = f32[16,32,1024]{2,0,1:T(8,128)S(1)} all-to-all(f32[16,32,1024]{2,0,1:T(8,128)S(1)} %bitcast.75), channel_id=1, replica_groups=mesh['fibre'=32,'group'=16] {'fibre'}, dimensions={1} | all-to-all | bytes 4194304 | tf_op jit(solution)/shard_map/all_to_all | solution.py:19
  126.2 4.6 convolution_multiply_fusion
  130.8 0.0 all-reduce.3.cloned.1.call-update
  130.8 0.2 all-reduce.5.cloned.1.call-start
  131.0 0.0 copy-done
  131.0 0.3 fusion.18
  131.3 0.1 copy.18
  131.4 5.8 %cholesky.74 = f32[64,64]{1,0:T(8,128)S(1)} custom-call(f32[64,64]{1,0:T(8,128)S(1)} %fusion.11), custom_call_target="Cholesky" | custom-call | tf_op jit(solution)/shard_map/jit(cholesky)/cholesky | solution.py:12
  137.3 101.7 %all-reduce.3.cloned.1.call-done = f32[512,512]{1,0:T(8,128)} async-done(((f32[512,512]{1,0:T(8,128)}), f32[512,512]{1,0:T(8,128)}) %all-reduce.3.cloned.1.call-update) | async-done | bytes 1048592 | tf_op jit(solution)/shard_map/psum | solution.py:23
  238.9 0.0 all-reduce.5.cloned.1.call-update
  239.0 0.6 compare_reduce_fusion.3
  239.6 0.7 fusion
  240.3 4.9 custom-call.8
  245.2 0.3 convolution_bitcast_fusion.3
  245.5 206.8 %all-reduce.5.cloned.1.call-done = f32[512,512]{1,0:T(8,128)} async-done(((f32[512,512]{1,0:T(8,128)}), f32[512,512]{1,0:T(8,128)}) %all-reduce.5.cloned.1.call-update) | async-done | bytes 1048592 | tf_op jit(solution)/shard_map/psum | solution.py:23
  452.3 0.0 copy-start.1
  452.3 2.4 fusion.19
  454.8 0.3 fusion.20
  455.0 0.1 copy.19
  455.1 5.8 %cholesky.85 = f32[64,64]{1,0:T(8,128)S(1)} custom-call(f32[64,64]{1,0:T(8,128)S(1)} %fusion.9), custom_call_target="Cholesky" | custom-call | tf_op jit(solution)/shard_map/jit(cholesky)/cholesky | solution.py:12
  461.0 0.6 compare_reduce_fusion.2
  461.6 0.7 fusion.1
  462.3 4.9 custom-call.9
  467.2 0.3 convolution_bitcast_fusion.2
  467.5 0.0 copy-done.1
  467.6 1.1 fusion.21
  468.7 0.3 fusion.22
  469.0 0.1 copy.20
  469.0 5.8 %cholesky.96 = f32[64,64]{1,0:T(8,128)S(1)} custom-call(f32[64,64]{1,0:T(8,128)S(1)} %fusion.7), custom_call_target="Cholesky" | custom-call | tf_op jit(solution)/shard_map/jit(cholesky)/cholesky | solution.py:12
  474.9 0.6 compare_reduce_fusion.1
  475.6 0.7 fusion.2
  476.2 4.9 custom-call.10
  481.1 0.3 convolution_bitcast_fusion.1
  481.5 1.1 fusion.23
  482.6 0.3 fusion.24
  482.9 0.1 copy.21
  483.0 5.8 %cholesky.107 = f32[64,64]{1,0:T(8,128)S(1)} custom-call(f32[64,64]{1,0:T(8,128)S(1)} %fusion.5), custom_call_target="Cholesky" | custom-call | tf_op jit(solution)/shard_map/jit(cholesky)/cholesky | solution.py:12
  488.9 0.6 compare_reduce_fusion
  489.5 0.7 fusion.3
  490.2 4.9 custom-call.11
  495.1 0.3 convolution_bitcast_fusion
  495.4 0.0 copy-start.2
  495.4 2.1 fusion.25
  497.5 0.0 copy-done.2
  (8 shorter events, 0.2 us)
Async XLA Ops:
  7.2 123.9 %copy-start = (f32[512,64]{0,1:T(8,128)S(1)}, f32[512,64]{0,1:T(8,128)}, u32[]{:S(2)}) copy-start(f32[512,64]{0,1:T(8,128)} %param.6) | copy-start | bytes 393220
  7.2 231.8 %all-reduce.3.cloned.1.call-start = ((), (), s32[]{:S(2)}) async-start(), calls=%async_computation.1 | async-start | bytes 2097152 | tf_op jit(solution)/shard_map/psum | solution.py:23
  130.8 321.5 %all-reduce.5.cloned.1.call-start = ((), (), s32[]{:S(2)}) async-start(), calls=%async_computation.2 | async-start | bytes 2097152 | tf_op jit(solution)/shard_map/psum | solution.py:23
  452.3 15.2 %copy-start.1 = (f32[512,512]{1,0:T(8,128)S(1)}, f32[512,512]{1,0:T(8,128)}, u32[]{:S(2)}) copy-start(f32[512,512]{1,0:T(8,128)} %all-reduce.5.cloned.1.call-done) | copy-start | bytes 3145732
  495.4 2.1 copy-start.2
Sparse Core Ops, SparseCore 0:
  130.9 107.9 all-reduce.2
  241.3 210.9 all-reduce.4
